TPU v7x, 128 devices: a whole 4x4x4 slice. The times are simulated.
128 devices in a mesh: region: 8 (over x, core), unit: 16 (over y, z).
Axes of the slice: x: 4, y: 4, z: 4, core: 2. Of those that a mesh axis runs over, the one named last changes fastest.
Arguments:
- noisy: bfloat16 [32768, 2048], P(('region', 'unit')), may hold values from -6 to 6
- strategy: bfloat16 [2048, 2048], replicated, may hold values from -0.125 to 0.125
- county_hist: float32 [1024, 2048], P(('region', 'unit')), may hold values from -24 to 24
- tract_county: int32 [32768], P(('region', 'unit')), may hold values from 0 to 1023, as said below
- tract_owner: int32 [32768, 1], P(('region', 'unit')), may hold values from 0 to 127; in each aligned block of 256 rows (0 to 255, 256 to 511, ...) at most 4 rows name the same one
Outputs:
- released: bfloat16 [32768, 2048], P(('region', 'unit'))
- relaid: float32 [65536, 2048], P(('region', 'unit'))
Inputs may be any that keep to these rules, and one draw needn't show every extreme that they name: `tract_county`: every county has at least one tract; the tracts of region r (rows r * 256 * 16 onward) lie in counties of region r (rows r * 8 * 16 onward of county_hist). `tract_owner`: among the 256 rows of one device no owner appears more than 4 times, and some owner appears exactly 4 times.
All inputs are finite; a program needn't handle non-finite values.
Results may differ from a plain program's by a relative error of at most 0.005.
Values sent between devices are 32-bit elements; how exact they have to be, the bound alone decides.
No kernel may reach another device: no remote copies, remote signals or barrier semaphores. Data moves between devices by JAX's collectives and lax.ppermute only.
A program may use at most 64 MiB of HBM per device.

v0:
```python
import jax
import jax.numpy as jnp
from jax import lax
from jax.sharding import PartitionSpec as P

ITERS = 2
step_size = 0.25


def local(noisy, strategy, county_hist, tract_county, tract_owner):
    unit_count = lax.axis_size("unit")
    region_count = lax.axis_size("region")
    devices = region_count * unit_count
    tract_rows = noisy.shape[0]
    width = strategy.shape[0]
    county_region = county_hist.shape[0] * unit_count
    first_county = lax.axis_index("region") * county_region
    local_id = tract_county - first_county
    member = (local_id[:, None] == jnp.arange(county_region, dtype=jnp.int32)[None, :]).astype(
        jnp.float32
    )
    county_tally = jnp.sum(member, axis=0)
    estimate = jnp.zeros((tract_rows, width), jnp.float32)
    for iteration in range(ITERS):
        if iteration == 0:
            misfit = -noisy
        else:
            answers = jnp.dot(
                estimate.astype(jnp.bfloat16), strategy, preferred_element_type=jnp.float32
            )
            misfit = (answers - noisy.astype(jnp.float32)).astype(jnp.bfloat16)
        gradient = lax.dot_general(
            misfit, strategy, (((1,), (1,)), ((), ())), preferred_element_type=jnp.float32
        )
        stepped = estimate - step_size * gradient
        partial_value = lax.dot_general(
            member,
            stepped,
            (((0,), (0,)), ((), ())),
            precision=lax.Precision.HIGHEST,
            preferred_element_type=jnp.float32,
        )
        child_total, tract_count = (
            lax.psum_scatter(partial_value, "unit", scatter_dimension=0, tiled=True),
            lax.psum_scatter(county_tally, "unit", scatter_dimension=0, tiled=True),
        )
        parent_gap = (county_hist - child_total) / tract_count[:, None]
        region_gap = lax.all_gather(parent_gap, "unit", axis=0, tiled=True)
        estimate = stepped + jnp.dot(
            member, region_gap, precision=lax.Precision.HIGHEST, preferred_element_type=jnp.float32
        )
    owners = tract_owner[:, 0]
    owner_hits = (owners[:, None] == jnp.arange(devices, dtype=jnp.int32)[None, :]).astype(
        jnp.int32
    )
    slot_index = jnp.sum((jnp.cumsum(owner_hits, axis=0) - owner_hits) * owner_hits, axis=1)
    capacity = 2 * tract_rows // devices
    target = owners * capacity + slot_index
    outgoing = jnp.zeros((devices * capacity, width), jnp.float32).at[target].set(estimate)
    released = jnp.dot(
        estimate.astype(jnp.bfloat16), strategy, preferred_element_type=jnp.float32
    ).astype(jnp.bfloat16)
    grouped = outgoing.reshape(devices, capacity, width)
    arrived = lax.all_to_all(grouped, ("region", "unit"), split_axis=0, concat_axis=0, tiled=True)
    relaid = arrived.reshape(devices * capacity, width)
    return (released, relaid)


def solution(mesh):
    in_specs = (
        P(("region", "unit"), None),
        P(),
        P(("region", "unit"), None),
        P(("region", "unit")),
        P(("region", "unit"), None),
    )
    out_specs = (P(("region", "unit"), None), P(("region", "unit"), None))
    return jax.shard_map(local, mesh=mesh, in_specs=in_specs, out_specs=out_specs, check_vma=False)
```

profile of v0, /device:TPU:6, one launch (start us, length us, event | category | flops | bytes accessed | tf_op | source)
XLA Modules:
  0.0 385.6 jit_solution(13782813712799772541)
XLA Ops:
  7.2 0.0 all-reduce.6.cloned.1.call-start
  7.2 0.7 broadcast_subtract_fusion
  7.9 6.1 %fusion = f32[256,2048]{1,0:T(8,128)S(1)} fusion(bf16[2048,2048]{1,0:T(8,128)(2,1)} %param.6, bf16[256,2048]{1,0:T(8,128)(2,1)} %param.5), kind=kOutput, calls=%fused_computation.5 | convolution fusion | flops 2149056512 | bytes 11534336 | tf_op jit(solution)/shard_map/dot_general | solution.py:32
  14.0 1.9 fusion.15
  15.9 0.0 all-reduce.6.cloned.1.call-update
  15.9 0.0 all-gather.3.cloned.1.call-start
  16.0 0.6 dynamic-slice
  17.2 0.1 convert_reduce_fusion
  17.4 42.1 %all-reduce.1 = f32[128]{0:T(128)S(1)} all-reduce(f32[128]{0:T(128)S(1)} %convert_reduce_fusion), channel_id=3, replica_groups=mesh['region'=8,'unit'=16] {'unit'}, use_global_device_ids=true, to_apply=%region_2.0.clone | all-reduce | flops 128 | bytes 1024
  59.4 0.1 dynamic-slice.3
  59.5 46.5 %all-reduce.6.cloned.1.call-done = f32[128,2048]{1,0:T(8,128)} async-done(((f32[128,2048]{1,0:T(8,128)}), f32[128,2048]{1,0:T(8,128)}) %all-reduce.6.cloned.1.call-update) | async-done | bytes 1048592
  106.0 1.5 fusion.17
  107.5 0.0 all-gather.3.cloned.1.call-update
  107.5 0.0 all-reduce.8.cloned.1.call-start
  107.6 42.9 %all-gather.3.cloned.1.call-done = f32[128,2048]{1,0:T(8,128)} async-done(((f32[8,2048]{1,0:T(8,128)}), f32[128,2048]{1,0:T(8,128)}) %all-gather.3.cloned.1.call-update) | async-done | bytes 1048592 | tf_op jit(solution)/shard_map/all_gather | solution.py:48
  150.5 3.6 convolution_add_fusion.1
  154.1 11.5 %fusion.1 = f32[256,2048]{1,0:T(8,128)S(1)} fusion(f32[256,2048]{1,0:T(8,128)} %convolution_add_fusion.1, bf16[2048,2048]{1,0:T(8,128)(2,1)} %param.6, bf16[256,2048]{1,0:T(8,128)(2,1)S(1)} %copy-done.3), kind=kOutput, calls=%fused_computation.6 | convolution fusion | flops 4298113024 | bytes 13631488 | tf_op jit(solution)/shard_map/dot_general | solution.py:32
  165.6 1.9 fusion.14
  167.5 0.2 all-gather.5.cloned.1.call-start
  167.7 86.7 %all-reduce.8.cloned.1.call-done = f32[128,2048]{1,0:T(8,128)} async-done(((f32[128,2048]{1,0:T(8,128)}), f32[128,2048]{1,0:T(8,128)}) %all-reduce.8.cloned.1.call-update) | async-done | bytes 1048592
  254.4 1.5 fusion.16
  256.0 0.1 copy.12
  256.1 0.2 fusion.10
  256.4 0.2 fusion.12
  256.6 42.2 %all-gather.5.cloned.1.call-done = f32[128,2048]{1,0:T(8,128)} async-done(((f32[8,2048]{1,0:T(8,128)}), f32[128,2048]{1,0:T(8,128)}) %all-gather.5.cloned.1.call-update) | async-done | bytes 1048592 | tf_op jit(solution)/shard_map/all_gather | solution.py:48
  298.8 3.6 convolution_add_fusion
  302.4 5.1 %scatter_custom_fusion = f32[512,2048]{1,0:T(8,128)} fusion(s32[256]{0:T(256)S(1)} %bitcast.33, f32[256,2048]{1,0:T(8,128)} %convolution_add_fusion, f32[]{:T(128)} %constant.8.clone.1), kind=kCustom, calls=%fused_computation.10 | custom fusion | bytes 4194816 | tf_op jit(solution)/shard_map/scatter | solution.py:59
  307.6 5.2 %reshape.30 = f32[128,4,2048]{2,1,0:T(4,128)} reshape(f32[512,2048]{1,0:T(8,128)} %scatter_custom_fusion) | data formatting | bytes 8388608 | tf_op jit(solution)/shard_map/reshape | solution.py:63
  312.7 7.8 %all-to-all-start = ((f32[128,4,2048]{2,1,0:T(4,128)}), f32[128,4,2048]{2,1,0:T(4,128)}, u32[]{:S(2)}, u32[]{:S(2)}) async-start(f32[128,4,2048]{2,1,0:T(4,128)} %reshape.30), calls=%async_computation | async-start | bytes 8388608 | tf_op jit(solution)/shard_map/all_to_all | solution.py:64
  320.6 6.7 %convolution_convert_fusion = bf16[256,2048]{1,0:T(8,128)(2,1)} fusion(bf16[2048,2048]{1,0:T(8,128)(2,1)} %param.6, f32[256,2048]{1,0:T(8,128)S(1)} %copy-done), kind=kOutput, calls=%fused_computation.9 | convolution fusion | flops 2148532224 | bytes 11534336 | tf_op jit(solution)/shard_map/dot_general | solution.py:60
  327.3 46.5 %all-to-all-done = f32[128,4,2048]{2,1,0:T(4,128)} async-done(((f32[128,4,2048]{2,1,0:T(4,128)}), f32[128,4,2048]{2,1,0:T(4,128)}, u32[]{:S(2)}, u32[]{:S(2)}) %all-to-all-start) | async-done | bytes 4194336 | tf_op jit(solution)/shard_map/all_to_all | solution.py:64
  373.8 5.3 %reshape.31 = f32[512,2048]{1,0:T(8,128)} reshape(f32[128,4,2048]{2,1,0:T(4,128)} %all-to-all-done) | data formatting | bytes 8388608 | tf_op jit(solution)/shard_map/reshape | solution.py:65
  (19 shorter events, 0.1 us)
Async XLA Ops:
  7.2 98.8 %all-reduce.6.cloned.1.call-start = ((), (), s32[]{:S(2)}) async-start(), calls=%async_computation.3 | async-start | bytes 2097152
  14.0 2.0 copy-start.4
  14.0 92.0 %copy-start.1 = (f32[8,2048]{1,0:T(8,128)S(1)}, f32[8,2048]{1,0:T(8,128)}, u32[]{:S(2)}) copy-start(f32[8,2048]{1,0:T(8,128)} %param.7) | copy-start | bytes 196612
  15.9 134.5 %all-gather.3.cloned.1.call-start = ((), (), s32[]{:S(2)}) async-start(), calls=%async_computation.1 | async-start | bytes 1114112 | tf_op jit(solution)/shard_map/all_gather | solution.py:48
  107.5 46.5 %copy-start.3 = (bf16[256,2048]{1,0:T(8,128)(2,1)S(1)}, bf16[256,2048]{1,0:T(8,128)(2,1)}, u32[]{:S(2)}) copy-start(bf16[256,2048]{1,0:T(8,128)(2,1)} %param.5) | copy-start | bytes 3145732
  107.5 146.9 %all-reduce.8.cloned.1.call-start = ((), (), s32[]{:S(2)}) async-start(), calls=%async_computation.4 | async-start | bytes 2097152
  165.6 90.4 %copy-start.2 = (s32[256,1]{0,1:T(1,128)S(1)}, s32[256,1]{0,1:T(1,128)}, u32[]{:S(2)}) copy-start(s32[256,1]{0,1:T(1,128)} %param.9) | copy-start | bytes 3076
  167.5 131.3 %all-gather.5.cloned.1.call-start = ((), (), s32[]{:S(2)}) async-start(), calls=%async_computation.2 | async-start | bytes 1114112 | tf_op jit(solution)/shard_map/all_gather | solution.py:48
  312.7 7.9 %copy-start = (f32[256,2048]{1,0:T(8,128)S(1)}, f32[256,2048]{1,0:T(8,128)}, u32[]{:S(2)}) copy-start(f32[256,2048]{1,0:T(8,128)} %convolution_add_fusion) | copy-start | bytes 6291460
  312.7 61.1 %all-to-all-start = ((f32[128,4,2048]{2,1,0:T(4,128)}), f32[128,4,2048]{2,1,0:T(4,128)}, u32[]{:S(2)}, u32[]{:S(2)}) async-start(f32[128,4,2048]{2,1,0:T(4,128)} %reshape.30), calls=%async_computation | async-start | bytes 8388608 | tf_op jit(solution)/shard_map/all_to_all | solution.py:64
Sparse Core Ops, SparseCore 0:
  16.1 89.8 all-reduce.5
  108.7 41.7 all-gather.2
  167.6 86.7 all-reduce.7
  257.0 41.7 all-gather.4
where the time goes:
time: 386 us
  waiting for transfers between devices  265 us (69%)
  blocking collectives  42.1 us (11%)
  matrix products  35.3 us (9%)
  local copies, waits for them, and re-layouts  16.4 us (4%)
  between operations  14.5 us (4%)
  starting transfers between devices  8.19 us (2%)
  other arithmetic  4.33 us (1%)
    unnamed x6, waiting for transfers between devices  133 us
    all_gather x2, waiting for transfers between devices, local(): region_gap = lax.all_gather(parent_gap, 'unit', axis=0, tiled=True)  85.1 us
    all_to_all x1, waiting for transfers between devices, local(): lax.all_to_all(grouped, ('region', 'unit'), split_axis=0, concat_axis=0,...  46.5 us
    unnamed x1, blocking collectives  42.1 us
    dot_general x2, matrix products, local(): lax.dot_general(misfit, strategy, (((1,), (1,)), ((), ())), preferred_ele...  17.6 us
    all_to_all x1, starting transfers between devices, local(): lax.all_to_all(grouped, ('region', 'unit'), split_axis=0, concat_axis=0,...  7.85 us
  transfers between devices with their start and end apart: 5, of which 5 were waited for; matrix products, arithmetic and copies ran while one was open for 2% of the time, Pallas kernels for 0%

commit v1 on v0

--- a/solution.py
+++ b/solution.py
@@ -5,6 +5,19 @@
 
 ITERS = 2
 step_size = 0.25
+
+
+def collect(x, axis, dim):
+    ways = lax.axis_size(axis)
+    up = [(d, (d + 1) % ways) for d in range(ways)]
+    down = [(d, (d - 1) % ways) for d in range(ways)]
+    earlier, later = ([x], [x])
+    for _ in range(ways // 2):
+        earlier.append(lax.ppermute(earlier[-1], axis, up))
+    for _ in range((ways - 1) // 2):
+        later.append(lax.ppermute(later[-1], axis, down))
+    line = jnp.concatenate([*earlier[::-1], *later[1:]], axis=dim)
+    return jnp.roll(line, (lax.axis_index(axis) - ways // 2) * x.shape[dim], axis=dim)
 
 
 def local(noisy, strategy, county_hist, tract_county, tract_owner):
@@ -45,7 +58,7 @@
             lax.psum_scatter(county_tally, "unit", scatter_dimension=0, tiled=True),
         )
         parent_gap = (county_hist - child_total) / tract_count[:, None]
-        region_gap = lax.all_gather(parent_gap, "unit", axis=0, tiled=True)
+        region_gap = collect(parent_gap, "unit", 0)
         estimate = stepped + jnp.dot(
             member, region_gap, precision=lax.Precision.HIGHEST, preferred_element_type=jnp.float32
         )

time: 386 us -> 424 us (1.098)
  starting transfers between devices: 8.19 us -> 89.6 us
  waiting for transfers between devices: 265 us -> 224 us
    all_gather x2 -> x0, waiting for transfers between devices: 85.1 us -> none  [local(): region_gap = lax.all_gather(parent_gap, 'unit', axis=0, tiled=True)]
    ppermute x0 -> x30, starting transfers between devices: none -> 79.6 us  [the longest x14 77.5 us: collect(): later.append(lax.ppermute(later[-1], axis, down))]
    ppermute x0 -> x30, waiting for transfers between devices: none -> 41.8 us  [the longest x16 41.3 us: collect(): earlier.append(lax.ppermute(earlier[-1], axis, up))]
    unnamed x6 -> x4, waiting for transfers between devices: 133 us -> 135 us
  transfers between devices with their start and end apart: 5 -> 33, of which waited for: 5 -> 23; matrix products, arithmetic and copies ran while one was open for 2% -> 2% of each run, Pallas kernels for 0% -> 0%
where the time goes in v1:
time: 424 us; the launch traced here: 423 us
  waiting for transfers between devices  224 us (53%)
  starting transfers between devices  89.6 us (21%)
  blocking collectives  42.1 us (10%)
  matrix products  33.3 us (8%)
  local copies, waits for them, and re-layouts  16.7 us (4%)
  between operations  15.1 us (4%)
    unnamed x4, waiting for transfers between devices  135 us
    ppermute x14, starting transfers between devices, collect(): later.append(lax.ppermute(later[-1], axis, down))  77.5 us
    all_to_all x1, waiting for transfers between devices, local(): lax.all_to_all(grouped, ('region', 'unit'), split_axis=0, concat_axis=0,...  46.5 us
    unnamed x1, blocking collectives  42.1 us
    ppermute x16, waiting for transfers between devices, collect(): earlier.append(lax.ppermute(earlier[-1], axis, up))  41.3 us
    dot_general x2, matrix products, local(): lax.dot_general(misfit, strategy, (((1,), (1,)), ((), ())), preferred_ele...  17.8 us
    all_to_all x1, starting transfers between devices, local(): lax.all_to_all(grouped, ('region', 'unit'), split_axis=0, concat_axis=0,...  9.96 us
  transfers between devices with their start and end apart: 33, of which 23 were waited for; matrix products, arithmetic and copies ran while one was open for 2% of the time, Pallas kernels for 0%

profile of v1, /device:TPU:6, one launch (start us, length us, event | category | flops | bytes accessed | tf_op | source)
XLA Modules:
  0.0 423.3 jit_solution(3994232389900689146)
XLA Ops:
  7.9 6.1 %fusion = f32[256,2048]{1,0:T(8,128)S(1)} fusion(bf16[2048,2048]{1,0:T(8,128)(2,1)} %param.8, bf16[256,2048]{1,0:T(8,128)(2,1)} %param.7), kind=kOutput, calls=%fused_computation.5 | convolution fusion | flops 2149056512 | bytes 11534336 | tf_op jit(solution)/shard_map/dot_general | solution.py:45
  17.4 42.1 %all-reduce.1 = f32[128]{0:T(128)S(1)} all-reduce(f32[128]{0:T(128)S(1)} %convert_reduce_fusion), channel_id=3, replica_groups=mesh['region'=8,'unit'=16] {'unit'}, use_global_device_ids=true, to_apply=%region_2.0.clone | all-reduce | flops 128 | bytes 1024
  59.5 46.5 %all-reduce.6.cloned.1.call-done = f32[128,2048]{1,0:T(8,128)} async-done(((f32[128,2048]{1,0:T(8,128)}), f32[128,2048]{1,0:T(8,128)}) %all-reduce.6.cloned.1.call-update) | async-done | bytes 1048592
  107.9 6.6 %collective-permute-done = f32[8,2048]{1,0:T(8,128)S(1)} collective-permute-done((f32[8,2048]{1,0:T(8,128)S(1)}, f32[8,2048]{1,0:T(8,128)S(1)}, u32[]{:S(2)}, u32[]{:S(2)}) %collective-permute-start) | collective-permute-done | bytes 65568 | tf_op jit(solution)/shard_map/ppermute | solution.py:16
  114.5 5.3 %collective-permute-start.8 = (f32[8,2048]{1,0:T(8,128)S(1)}, f32[8,2048]{1,0:T(8,128)S(1)}, u32[]{:S(2)}, u32[]{:S(2)}) collective-permute-start(f32[8,2048]{1,0:T(8,128)S(1)} %fusion.21), channel_id=1, source_target_pairs={{0,15},{1,0},{2,1},{3,2},{4,3},{5,4},{6,5},{7,6},{8,7},{9,8},{10,9... | collective-permute-start | bytes 196616 | tf_op jit(solution)/shard_map/ppermute | solution.py:18
  119.8 2.2 collective-permute-done.1
  122.1 5.3 %collective-permute-start.9 = (f32[8,2048]{1,0:T(8,128)S(1)}, f32[8,2048]{1,0:T(8,128)S(1)}, u32[]{:S(2)}, u32[]{:S(2)}) collective-permute-start(f32[8,2048]{1,0:T(8,128)S(1)} %collective-permute-done.8), channel_id=1, source_target_pairs={{0,15},{1,0},{2,1},{3,2},{4,3},{5,4},{6,5},{7,6},{8,7},{9,8},{10,9... | collective-permute-start | bytes 196616 | tf_op jit(solution)/shard_map/ppermute | solution.py:18
  129.6 5.3 %collective-permute-start.10 = (f32[8,2048]{1,0:T(8,128)S(1)}, f32[8,2048]{1,0:T(8,128)S(1)}, u32[]{:S(2)}, u32[]{:S(2)}) collective-permute-start(f32[8,2048]{1,0:T(8,128)S(1)} %collective-permute-done.9), channel_id=1, source_target_pairs={{0,15},{1,0},{2,1},{3,2},{4,3},{5,4},{6,5},{7,6},{8,7},{9,8},{10,9... | collective-permute-start | bytes 196616 | tf_op jit(solution)/shard_map/ppermute | solution.py:18
  135.0 2.5 collective-permute-done.3
  137.5 5.6 %collective-permute-start.11 = (f32[8,2048]{1,0:T(8,128)S(1)}, f32[8,2048]{1,0:T(8,128)S(1)}, u32[]{:S(2)}, u32[]{:S(2)}) collective-permute-start(f32[8,2048]{1,0:T(8,128)S(1)} %collective-permute-done.10), channel_id=1, source_target_pairs={{0,15},{1,0},{2,1},{3,2},{4,3},{5,4},{6,5},{7,6},{8,7},{9,8},{10,9... | collective-permute-start | bytes 196616 | tf_op jit(solution)/shard_map/ppermute | solution.py:18
  145.1 5.6 %collective-permute-start.12 = (f32[8,2048]{1,0:T(8,128)S(1)}, f32[8,2048]{1,0:T(8,128)S(1)}, u32[]{:S(2)}, u32[]{:S(2)}) collective-permute-start(f32[8,2048]{1,0:T(8,128)S(1)} %collective-permute-done.11), channel_id=1, source_target_pairs={{0,15},{1,0},{2,1},{3,2},{4,3},{5,4},{6,5},{7,6},{8,7},{9,8},{10,9... | collective-permute-start | bytes 196616 | tf_op jit(solution)/shard_map/ppermute | solution.py:18
  152.7 5.6 %collective-permute-start.13 = (f32[8,2048]{1,0:T(8,128)S(1)}, f32[8,2048]{1,0:T(8,128)S(1)}, u32[]{:S(2)}, u32[]{:S(2)}) collective-permute-start(f32[8,2048]{1,0:T(8,128)S(1)} %collective-permute-done.12), channel_id=1, source_target_pairs={{0,15},{1,0},{2,1},{3,2},{4,3},{5,4},{6,5},{7,6},{8,7},{9,8},{10,9... | collective-permute-start | bytes 196616 | tf_op jit(solution)/shard_map/ppermute | solution.py:18
  160.3 5.6 %collective-permute-start.14 = (f32[8,2048]{1,0:T(8,128)S(1)}, f32[8,2048]{1,0:T(8,128)S(1)}, u32[]{:S(2)}, u32[]{:S(2)}) collective-permute-start(f32[8,2048]{1,0:T(8,128)S(1)} %collective-permute-done.13), channel_id=1, source_target_pairs={{0,15},{1,0},{2,1},{3,2},{4,3},{5,4},{6,5},{7,6},{8,7},{9,8},{10,9... | collective-permute-start | bytes 196616 | tf_op jit(solution)/shard_map/ppermute | solution.py:18
  168.1 2.4 convolution_add_fusion.1
  170.5 11.8 %fusion.1 = f32[256,2048]{1,0:T(8,128)S(1)} fusion(f32[256,2048]{1,0:T(8,128)} %convolution_add_fusion.1, bf16[2048,2048]{1,0:T(8,128)(2,1)} %param.8, bf16[256,2048]{1,0:T(8,128)(2,1)} %param.7), kind=kOutput, calls=%fused_computation.6 | convolution fusion | flops 4298113024 | bytes 13631488 | tf_op jit(solution)/shard_map/dot_general | solution.py:45
  184.3 88.8 %all-reduce.8.cloned.1.call-done = f32[128,2048]{1,0:T(8,128)} async-done(((f32[128,2048]{1,0:T(8,128)}), f32[128,2048]{1,0:T(8,128)}) %all-reduce.8.cloned.1.call-update) | async-done | bytes 1048592
  274.9 6.6 %collective-permute-done.15 = f32[8,2048]{1,0:T(8,128)S(1)} collective-permute-done((f32[8,2048]{1,0:T(8,128)S(1)}, f32[8,2048]{1,0:T(8,128)S(1)}, u32[]{:S(2)}, u32[]{:S(2)}) %collective-permute-start.15) | collective-permute-done | bytes 65568 | tf_op jit(solution)/shard_map/ppermute | solution.py:16
  281.5 5.3 %collective-permute-start.23 = (f32[8,2048]{1,0:T(8,128)S(1)}, f32[8,2048]{1,0:T(8,128)S(1)}, u32[]{:S(2)}, u32[]{:S(2)}) collective-permute-start(f32[8,2048]{1,0:T(8,128)S(1)} %fusion.20), channel_id=1, source_target_pairs={{0,15},{1,0},{2,1},{3,2},{4,3},{5,4},{6,5},{7,6},{8,7},{9,8},{10,9... | collective-permute-start | bytes 196616 | tf_op jit(solution)/shard_map/ppermute | solution.py:18
  289.2 5.4 %collective-permute-start.24 = (f32[8,2048]{1,0:T(8,128)S(1)}, f32[8,2048]{1,0:T(8,128)S(1)}, u32[]{:S(2)}, u32[]{:S(2)}) collective-permute-start(f32[8,2048]{1,0:T(8,128)S(1)} %collective-permute-done.23), channel_id=1, source_target_pairs={{0,15},{1,0},{2,1},{3,2},{4,3},{5,4},{6,5},{7,6},{8,7},{9,8},{10,9... | collective-permute-start | bytes 196616 | tf_op jit(solution)/shard_map/ppermute | solution.py:18
  296.9 5.4 %collective-permute-start.25 = (f32[8,2048]{1,0:T(8,128)S(1)}, f32[8,2048]{1,0:T(8,128)S(1)}, u32[]{:S(2)}, u32[]{:S(2)}) collective-permute-start(f32[8,2048]{1,0:T(8,128)S(1)} %collective-permute-done.24), channel_id=1, source_target_pairs={{0,15},{1,0},{2,1},{3,2},{4,3},{5,4},{6,5},{7,6},{8,7},{9,8},{10,9... | collective-permute-start | bytes 196616 | tf_op jit(solution)/shard_map/ppermute | solution.py:18
  302.3 2.3 collective-permute-done.18
  304.7 5.8 %collective-permute-start.26 = (f32[8,2048]{1,0:T(8,128)S(1)}, f32[8,2048]{1,0:T(8,128)S(1)}, u32[]{:S(2)}, u32[]{:S(2)}) collective-permute-start(f32[8,2048]{1,0:T(8,128)S(1)} %collective-permute-done.25), channel_id=1, source_target_pairs={{0,15},{1,0},{2,1},{3,2},{4,3},{5,4},{6,5},{7,6},{8,7},{9,8},{10,9... | collective-permute-start | bytes 196616 | tf_op jit(solution)/shard_map/ppermute | solution.py:18
  312.4 5.7 %collective-permute-start.27 = (f32[8,2048]{1,0:T(8,128)S(1)}, f32[8,2048]{1,0:T(8,128)S(1)}, u32[]{:S(2)}, u32[]{:S(2)}) collective-permute-start(f32[8,2048]{1,0:T(8,128)S(1)} %collective-permute-done.26), channel_id=1, source_target_pairs={{0,15},{1,0},{2,1},{3,2},{4,3},{5,4},{6,5},{7,6},{8,7},{9,8},{10,9... | collective-permute-start | bytes 196616 | tf_op jit(solution)/shard_map/ppermute | solution.py:18
  320.0 5.7 %collective-permute-start.28 = (f32[8,2048]{1,0:T(8,128)S(1)}, f32[8,2048]{1,0:T(8,128)S(1)}, u32[]{:S(2)}, u32[]{:S(2)}) collective-permute-start(f32[8,2048]{1,0:T(8,128)S(1)} %collective-permute-done.27), channel_id=1, source_target_pairs={{0,15},{1,0},{2,1},{3,2},{4,3},{5,4},{6,5},{7,6},{8,7},{9,8},{10,9... | collective-permute-start | bytes 196616 | tf_op jit(solution)/shard_map/ppermute | solution.py:18
  327.6 5.7 %collective-permute-start.29 = (f32[8,2048]{1,0:T(8,128)S(1)}, f32[8,2048]{1,0:T(8,128)S(1)}, u32[]{:S(2)}, u32[]{:S(2)}) collective-permute-start(f32[8,2048]{1,0:T(8,128)S(1)} %collective-permute-done.28), channel_id=1, source_target_pairs={{0,15},{1,0},{2,1},{3,2},{4,3},{5,4},{6,5},{7,6},{8,7},{9,8},{10,9... | collective-permute-start | bytes 196616 | tf_op jit(solution)/shard_map/ppermute | solution.py:18
  335.2 2.5 convolution_add_fusion
  337.7 5.1 %scatter_custom_fusion = f32[512,2048]{1,0:T(8,128)} fusion(s32[256]{0:T(256)S(1)} %bitcast.31, f32[256,2048]{1,0:T(8,128)} %convolution_add_fusion, f32[]{:T(128)} %constant.38.clone.1), kind=kCustom, calls=%fused_computation.14 | custom fusion | bytes 4194816 | tf_op jit(solution)/shard_map/scatter | solution.py:72
  342.8 5.2 %reshape.30 = f32[128,4,2048]{2,1,0:T(4,128)} reshape(f32[512,2048]{1,0:T(8,128)} %scatter_custom_fusion) | data formatting | bytes 8388608 | tf_op jit(solution)/shard_map/reshape | solution.py:76
  348.0 10.0 %all-to-all-start = ((f32[128,4,2048]{2,1,0:T(4,128)}), f32[128,4,2048]{2,1,0:T(4,128)}, u32[]{:S(2)}, u32[]{:S(2)}) async-start(f32[128,4,2048]{2,1,0:T(4,128)} %reshape.30), calls=%async_computation | async-start | bytes 8388608 | tf_op jit(solution)/shard_map/all_to_all | solution.py:77
  358.0 6.7 %convolution_convert_fusion = bf16[256,2048]{1,0:T(8,128)(2,1)} fusion(bf16[2048,2048]{1,0:T(8,128)(2,1)} %param.8, f32[256,2048]{1,0:T(8,128)S(1)} %copy-done), kind=kOutput, calls=%fused_computation.9 | convolution fusion | flops 2148532224 | bytes 11534336 | tf_op jit(solution)/shard_map/dot_general | solution.py:73
  364.7 46.5 %all-to-all-done = f32[128,4,2048]{2,1,0:T(4,128)} async-done(((f32[128,4,2048]{2,1,0:T(4,128)}), f32[128,4,2048]{2,1,0:T(4,128)}, u32[]{:S(2)}, u32[]{:S(2)}) %all-to-all-start) | async-done | bytes 4194336 | tf_op jit(solution)/shard_map/all_to_all | solution.py:77
  411.2 5.3 %reshape.31 = f32[512,2048]{1,0:T(8,128)} reshape(f32[128,4,2048]{2,1,0:T(4,128)} %all-to-all-done) | data formatting | bytes 8388608 | tf_op jit(solution)/shard_map/reshape | solution.py:78
  (103 shorter events, 31.7 us)
Async XLA Ops:
  7.2 98.8 %all-reduce.6.cloned.1.call-start = ((), (), s32[]{:S(2)}) async-start(), calls=%async_computation.1 | async-start | bytes 2097152
  15.9 257.1 %all-reduce.8.cloned.1.call-start = ((), (), s32[]{:S(2)}) async-start(), calls=%async_computation.2 | async-start | bytes 2097152
  106.9 7.6 %collective-permute-start = (f32[8,2048]{1,0:T(8,128)S(1)}, f32[8,2048]{1,0:T(8,128)S(1)}, u32[]{:S(2)}, u32[]{:S(2)}) collective-permute-start(f32[8,2048]{1,0:T(8,128)S(1)} %fusion.21), channel_id=1, source_target_pairs={{0,1},{1,2},{2,3},{3,4},{4,5},{5,6},{6,7},{7,8},{8,9},{9,10},{10,1... | collective-permute-start | bytes 196616 | tf_op jit(solution)/shard_map/ppermute | solution.py:16
  114.5 7.6 %collective-permute-start.1 = (f32[8,2048]{1,0:T(8,128)S(1)}, f32[8,2048]{1,0:T(8,128)S(1)}, u32[]{:S(2)}, u32[]{:S(2)}) collective-permute-start(f32[8,2048]{1,0:T(8,128)S(1)} %collective-permute-done), channel_id=1, source_target_pairs={{0,1},{1,2},{2,3},{3,4},{4,5},{5,6},{6,7},{7,8},{8,9},{9,10},{10,1... | collective-permute-start | bytes 196616 | tf_op jit(solution)/shard_map/ppermute | solution.py:16
  114.5 7.6 %collective-permute-start.8 = (f32[8,2048]{1,0:T(8,128)S(1)}, f32[8,2048]{1,0:T(8,128)S(1)}, u32[]{:S(2)}, u32[]{:S(2)}) collective-permute-start(f32[8,2048]{1,0:T(8,128)S(1)} %fusion.21), channel_id=1, source_target_pairs={{0,15},{1,0},{2,1},{3,2},{4,3},{5,4},{6,5},{7,6},{8,7},{9,8},{10,9... | collective-permute-start | bytes 196616 | tf_op jit(solution)/shard_map/ppermute | solution.py:18
  122.1 7.6 %collective-permute-start.2 = (f32[8,2048]{1,0:T(8,128)S(1)}, f32[8,2048]{1,0:T(8,128)S(1)}, u32[]{:S(2)}, u32[]{:S(2)}) collective-permute-start(f32[8,2048]{1,0:T(8,128)S(1)} %collective-permute-done.1), channel_id=1, source_target_pairs={{0,1},{1,2},{2,3},{3,4},{4,5},{5,6},{6,7},{7,8},{8,9},{9,10},{10,1... | collective-permute-start | bytes 196616 | tf_op jit(solution)/shard_map/ppermute | solution.py:16
  122.1 7.6 %collective-permute-start.9 = (f32[8,2048]{1,0:T(8,128)S(1)}, f32[8,2048]{1,0:T(8,128)S(1)}, u32[]{:S(2)}, u32[]{:S(2)}) collective-permute-start(f32[8,2048]{1,0:T(8,128)S(1)} %collective-permute-done.8), channel_id=1, source_target_pairs={{0,15},{1,0},{2,1},{3,2},{4,3},{5,4},{6,5},{7,6},{8,7},{9,8},{10,9... | collective-permute-start | bytes 196616 | tf_op jit(solution)/shard_map/ppermute | solution.py:18
  129.6 7.9 %collective-permute-start.3 = (f32[8,2048]{1,0:T(8,128)S(1)}, f32[8,2048]{1,0:T(8,128)S(1)}, u32[]{:S(2)}, u32[]{:S(2)}) collective-permute-start(f32[8,2048]{1,0:T(8,128)S(1)} %collective-permute-done.2), channel_id=1, source_target_pairs={{0,1},{1,2},{2,3},{3,4},{4,5},{5,6},{6,7},{7,8},{8,9},{9,10},{10,1... | collective-permute-start | bytes 196616 | tf_op jit(solution)/shard_map/ppermute | solution.py:16
  129.6 7.9 %collective-permute-start.10 = (f32[8,2048]{1,0:T(8,128)S(1)}, f32[8,2048]{1,0:T(8,128)S(1)}, u32[]{:S(2)}, u32[]{:S(2)}) collective-permute-start(f32[8,2048]{1,0:T(8,128)S(1)} %collective-permute-done.9), channel_id=1, source_target_pairs={{0,15},{1,0},{2,1},{3,2},{4,3},{5,4},{6,5},{7,6},{8,7},{9,8},{10,9... | collective-permute-start | bytes 196616 | tf_op jit(solution)/shard_map/ppermute | solution.py:18
  137.5 7.6 %collective-permute-start.4 = (f32[8,2048]{1,0:T(8,128)S(1)}, f32[8,2048]{1,0:T(8,128)S(1)}, u32[]{:S(2)}, u32[]{:S(2)}) collective-permute-start(f32[8,2048]{1,0:T(8,128)S(1)} %collective-permute-done.3), channel_id=1, source_target_pairs={{0,1},{1,2},{2,3},{3,4},{4,5},{5,6},{6,7},{7,8},{8,9},{9,10},{10,1... | collective-permute-start | bytes 196616 | tf_op jit(solution)/shard_map/ppermute | solution.py:16
  137.5 7.6 %collective-permute-start.11 = (f32[8,2048]{1,0:T(8,128)S(1)}, f32[8,2048]{1,0:T(8,128)S(1)}, u32[]{:S(2)}, u32[]{:S(2)}) collective-permute-start(f32[8,2048]{1,0:T(8,128)S(1)} %collective-permute-done.10), channel_id=1, source_target_pairs={{0,15},{1,0},{2,1},{3,2},{4,3},{5,4},{6,5},{7,6},{8,7},{9,8},{10,9... | collective-permute-start | bytes 196616 | tf_op jit(solution)/shard_map/ppermute | solution.py:18
  145.1 7.6 %collective-permute-start.5 = (f32[8,2048]{1,0:T(8,128)S(1)}, f32[8,2048]{1,0:T(8,128)S(1)}, u32[]{:S(2)}, u32[]{:S(2)}) collective-permute-start(f32[8,2048]{1,0:T(8,128)S(1)} %collective-permute-done.4), channel_id=1, source_target_pairs={{0,1},{1,2},{2,3},{3,4},{4,5},{5,6},{6,7},{7,8},{8,9},{9,10},{10,1... | collective-permute-start | bytes 196616 | tf_op jit(solution)/shard_map/ppermute | solution.py:16
  145.1 7.6 %collective-permute-start.12 = (f32[8,2048]{1,0:T(8,128)S(1)}, f32[8,2048]{1,0:T(8,128)S(1)}, u32[]{:S(2)}, u32[]{:S(2)}) collective-permute-start(f32[8,2048]{1,0:T(8,128)S(1)} %collective-permute-done.11), channel_id=1, source_target_pairs={{0,15},{1,0},{2,1},{3,2},{4,3},{5,4},{6,5},{7,6},{8,7},{9,8},{10,9... | collective-permute-start | bytes 196616 | tf_op jit(solution)/shard_map/ppermute | solution.py:18
  152.7 7.6 %collective-permute-start.6 = (f32[8,2048]{1,0:T(8,128)S(1)}, f32[8,2048]{1,0:T(8,128)S(1)}, u32[]{:S(2)}, u32[]{:S(2)}) collective-permute-start(f32[8,2048]{1,0:T(8,128)S(1)} %collective-permute-done.5), channel_id=1, source_target_pairs={{0,1},{1,2},{2,3},{3,4},{4,5},{5,6},{6,7},{7,8},{8,9},{9,10},{10,1... | collective-permute-start | bytes 196616 | tf_op jit(solution)/shard_map/ppermute | solution.py:16
  152.7 7.6 %collective-permute-start.13 = (f32[8,2048]{1,0:T(8,128)S(1)}, f32[8,2048]{1,0:T(8,128)S(1)}, u32[]{:S(2)}, u32[]{:S(2)}) collective-permute-start(f32[8,2048]{1,0:T(8,128)S(1)} %collective-permute-done.12), channel_id=1, source_target_pairs={{0,15},{1,0},{2,1},{3,2},{4,3},{5,4},{6,5},{7,6},{8,7},{9,8},{10,9... | collective-permute-start | bytes 196616 | tf_op jit(solution)/shard_map/ppermute | solution.py:18
  160.3 7.6 %collective-permute-start.7 = (f32[8,2048]{1,0:T(8,128)S(1)}, f32[8,2048]{1,0:T(8,128)S(1)}, u32[]{:S(2)}, u32[]{:S(2)}) collective-permute-start(f32[8,2048]{1,0:T(8,128)S(1)} %collective-permute-done.6), channel_id=1, source_target_pairs={{0,1},{1,2},{2,3},{3,4},{4,5},{5,6},{6,7},{7,8},{8,9},{9,10},{10,1... | collective-permute-start | bytes 196616 | tf_op jit(solution)/shard_map/ppermute | solution.py:16
  160.3 7.8 %collective-permute-start.14 = (f32[8,2048]{1,0:T(8,128)S(1)}, f32[8,2048]{1,0:T(8,128)S(1)}, u32[]{:S(2)}, u32[]{:S(2)}) collective-permute-start(f32[8,2048]{1,0:T(8,128)S(1)} %collective-permute-done.13), channel_id=1, source_target_pairs={{0,15},{1,0},{2,1},{3,2},{4,3},{5,4},{6,5},{7,6},{8,7},{9,8},{10,9... | collective-permute-start | bytes 196616 | tf_op jit(solution)/shard_map/ppermute | solution.py:18
  273.9 7.6 %collective-permute-start.15 = (f32[8,2048]{1,0:T(8,128)S(1)}, f32[8,2048]{1,0:T(8,128)S(1)}, u32[]{:S(2)}, u32[]{:S(2)}) collective-permute-start(f32[8,2048]{1,0:T(8,128)S(1)} %fusion.20), channel_id=1, source_target_pairs={{0,1},{1,2},{2,3},{3,4},{4,5},{5,6},{6,7},{7,8},{8,9},{9,10},{10,1... | collective-permute-start | bytes 196616 | tf_op jit(solution)/shard_map/ppermute | solution.py:16
  281.5 7.6 %collective-permute-start.16 = (f32[8,2048]{1,0:T(8,128)S(1)}, f32[8,2048]{1,0:T(8,128)S(1)}, u32[]{:S(2)}, u32[]{:S(2)}) collective-permute-start(f32[8,2048]{1,0:T(8,128)S(1)} %collective-permute-done.15), channel_id=1, source_target_pairs={{0,1},{1,2},{2,3},{3,4},{4,5},{5,6},{6,7},{7,8},{8,9},{9,10},{10,1... | collective-permute-start | bytes 196616 | tf_op jit(solution)/shard_map/ppermute | solution.py:16
  281.5 7.7 %collective-permute-start.23 = (f32[8,2048]{1,0:T(8,128)S(1)}, f32[8,2048]{1,0:T(8,128)S(1)}, u32[]{:S(2)}, u32[]{:S(2)}) collective-permute-start(f32[8,2048]{1,0:T(8,128)S(1)} %fusion.20), channel_id=1, source_target_pairs={{0,15},{1,0},{2,1},{3,2},{4,3},{5,4},{6,5},{7,6},{8,7},{9,8},{10,9... | collective-permute-start | bytes 196616 | tf_op jit(solution)/shard_map/ppermute | solution.py:18
  289.1 7.6 %collective-permute-start.17 = (f32[8,2048]{1,0:T(8,128)S(1)}, f32[8,2048]{1,0:T(8,128)S(1)}, u32[]{:S(2)}, u32[]{:S(2)}) collective-permute-start(f32[8,2048]{1,0:T(8,128)S(1)} %collective-permute-done.16), channel_id=1, source_target_pairs={{0,1},{1,2},{2,3},{3,4},{4,5},{5,6},{6,7},{7,8},{8,9},{9,10},{10,1... | collective-permute-start | bytes 196616 | tf_op jit(solution)/shard_map/ppermute | solution.py:16
  289.2 7.7 %collective-permute-start.24 = (f32[8,2048]{1,0:T(8,128)S(1)}, f32[8,2048]{1,0:T(8,128)S(1)}, u32[]{:S(2)}, u32[]{:S(2)}) collective-permute-start(f32[8,2048]{1,0:T(8,128)S(1)} %collective-permute-done.23), channel_id=1, source_target_pairs={{0,15},{1,0},{2,1},{3,2},{4,3},{5,4},{6,5},{7,6},{8,7},{9,8},{10,9... | collective-permute-start | bytes 196616 | tf_op jit(solution)/shard_map/ppermute | solution.py:18
  296.7 7.9 %collective-permute-start.18 = (f32[8,2048]{1,0:T(8,128)S(1)}, f32[8,2048]{1,0:T(8,128)S(1)}, u32[]{:S(2)}, u32[]{:S(2)}) collective-permute-start(f32[8,2048]{1,0:T(8,128)S(1)} %collective-permute-done.17), channel_id=1, source_target_pairs={{0,1},{1,2},{2,3},{3,4},{4,5},{5,6},{6,7},{7,8},{8,9},{9,10},{10,1... | collective-permute-start | bytes 196616 | tf_op jit(solution)/shard_map/ppermute | solution.py:16
  296.9 7.8 %collective-permute-start.25 = (f32[8,2048]{1,0:T(8,128)S(1)}, f32[8,2048]{1,0:T(8,128)S(1)}, u32[]{:S(2)}, u32[]{:S(2)}) collective-permute-start(f32[8,2048]{1,0:T(8,128)S(1)} %collective-permute-done.24), channel_id=1, source_target_pairs={{0,15},{1,0},{2,1},{3,2},{4,3},{5,4},{6,5},{7,6},{8,7},{9,8},{10,9... | collective-permute-start | bytes 196616 | tf_op jit(solution)/shard_map/ppermute | solution.py:18
  304.6 7.6 %collective-permute-start.19 = (f32[8,2048]{1,0:T(8,128)S(1)}, f32[8,2048]{1,0:T(8,128)S(1)}, u32[]{:S(2)}, u32[]{:S(2)}) collective-permute-start(f32[8,2048]{1,0:T(8,128)S(1)} %collective-permute-done.18), channel_id=1, source_target_pairs={{0,1},{1,2},{2,3},{3,4},{4,5},{5,6},{6,7},{7,8},{8,9},{9,10},{10,1... | collective-permute-start | bytes 196616 | tf_op jit(solution)/shard_map/ppermute | solution.py:16
  304.7 7.7 %collective-permute-start.26 = (f32[8,2048]{1,0:T(8,128)S(1)}, f32[8,2048]{1,0:T(8,128)S(1)}, u32[]{:S(2)}, u32[]{:S(2)}) collective-permute-start(f32[8,2048]{1,0:T(8,128)S(1)} %collective-permute-done.25), channel_id=1, source_target_pairs={{0,15},{1,0},{2,1},{3,2},{4,3},{5,4},{6,5},{7,6},{8,7},{9,8},{10,9... | collective-permute-start | bytes 196616 | tf_op jit(solution)/shard_map/ppermute | solution.py:18
  312.2 7.6 %collective-permute-start.20 = (f32[8,2048]{1,0:T(8,128)S(1)}, f32[8,2048]{1,0:T(8,128)S(1)}, u32[]{:S(2)}, u32[]{:S(2)}) collective-permute-start(f32[8,2048]{1,0:T(8,128)S(1)} %collective-permute-done.19), channel_id=1, source_target_pairs={{0,1},{1,2},{2,3},{3,4},{4,5},{5,6},{6,7},{7,8},{8,9},{9,10},{10,1... | collective-permute-start | bytes 196616 | tf_op jit(solution)/shard_map/ppermute | solution.py:16
  312.4 7.6 %collective-permute-start.27 = (f32[8,2048]{1,0:T(8,128)S(1)}, f32[8,2048]{1,0:T(8,128)S(1)}, u32[]{:S(2)}, u32[]{:S(2)}) collective-permute-start(f32[8,2048]{1,0:T(8,128)S(1)} %collective-permute-done.26), channel_id=1, source_target_pairs={{0,15},{1,0},{2,1},{3,2},{4,3},{5,4},{6,5},{7,6},{8,7},{9,8},{10,9... | collective-permute-start | bytes 196616 | tf_op jit(solution)/shard_map/ppermute | solution.py:18
  319.8 7.6 %collective-permute-start.21 = (f32[8,2048]{1,0:T(8,128)S(1)}, f32[8,2048]{1,0:T(8,128)S(1)}, u32[]{:S(2)}, u32[]{:S(2)}) collective-permute-start(f32[8,2048]{1,0:T(8,128)S(1)} %collective-permute-done.20), channel_id=1, source_target_pairs={{0,1},{1,2},{2,3},{3,4},{4,5},{5,6},{6,7},{7,8},{8,9},{9,10},{10,1... | collective-permute-start | bytes 196616 | tf_op jit(solution)/shard_map/ppermute | solution.py:16
  327.4 7.6 %collective-permute-start.22 = (f32[8,2048]{1,0:T(8,128)S(1)}, f32[8,2048]{1,0:T(8,128)S(1)}, u32[]{:S(2)}, u32[]{:S(2)}) collective-permute-start(f32[8,2048]{1,0:T(8,128)S(1)} %collective-permute-done.21), channel_id=1, source_target_pairs={{0,1},{1,2},{2,3},{3,4},{4,5},{5,6},{6,7},{7,8},{8,9},{9,10},{10,1... | collective-permute-start | bytes 196616 | tf_op jit(solution)/shard_map/ppermute | solution.py:16
  327.6 7.6 %collective-permute-start.29 = (f32[8,2048]{1,0:T(8,128)S(1)}, f32[8,2048]{1,0:T(8,128)S(1)}, u32[]{:S(2)}, u32[]{:S(2)}) collective-permute-start(f32[8,2048]{1,0:T(8,128)S(1)} %collective-permute-done.28), channel_id=1, source_target_pairs={{0,15},{1,0},{2,1},{3,2},{4,3},{5,4},{6,5},{7,6},{8,7},{9,8},{10,9... | collective-permute-start | bytes 196616 | tf_op jit(solution)/shard_map/ppermute | solution.py:18
  348.0 63.2 %all-to-all-start = ((f32[128,4,2048]{2,1,0:T(4,128)}), f32[128,4,2048]{2,1,0:T(4,128)}, u32[]{:S(2)}, u32[]{:S(2)}) async-start(f32[128,4,2048]{2,1,0:T(4,128)} %reshape.30), calls=%async_computation | async-start | bytes 8388608 | tf_op jit(solution)/shard_map/all_to_all | solution.py:77
  (5 other events, 218.3 us)
Sparse Core Ops, SparseCore 0:
  16.1 89.8 all-reduce.5
  184.4 88.5 all-reduce.7
